TPU v7x, 256 devices: a whole 4x4x8 slice. The times are simulated.
256 devices in a mesh: dp: 8 (over y, core), tm: 32 (over z, x).
Axes of the slice: x: 4, y: 4, z: 8, core: 2. Of those that a mesh axis runs over, the one named last changes fastest.
Arguments:
- window: bfloat16 [1024, 512, 512], P('tm', 'dp'), may hold values from -6 to 6
- link_ids: int32 [1024, 512], P('tm', 'dp'), may hold values from 0 to 63
- knot_ids: int32 [1024, 512], P('tm', 'dp'), may hold values from 0 to 511, as said below
- lag_steps: int32 [4], replicated, may hold values from 1 to 7, as said below
- topology: int32 [64, 64], replicated, may hold values 0 or 1
- smooth: float32 [256], replicated, may hold values from 200 to 6000
Outputs:
- scaled_coefs: float32 [512, 256], P(('dp', 'tm'))
Inputs may be any that keep to these rules, and one draw needn't show every extreme that they name: `knot_ids`: the sample in row a and column b of the sample grid belongs to a knot k with k // 64 = (b % 64) // 8 and (k % 64) // 2 = a // 32: each device's columns come in 8 blocks of 8, block i holding samples of knots of the i-th index of dp. `lag_steps`: the lags are distinct; 1 and 7 are among them.
All inputs are finite; a program needn't handle non-finite values.
Results may differ from a plain program's by a relative error of at most 0.0019.
Values may be sent and summed in bfloat16 or wider, within the bound.
No kernel may reach another device: no remote copies, remote signals or barrier semaphores. Data moves between devices by JAX's collectives and lax.ppermute only.
A program may use at most 128 MiB of HBM per device.

v0:
```python
import jax
import jax.numpy as jnp
from jax import lax
from jax.sharding import PartitionSpec as P

GROUPS = 64
NLAG = 4
WIN = 8
KPD = 2


RIDGE_TERM = 0.1


def from_behind(block, axis, distance):
    devices = range(lax.axis_size(axis))
    route = [(i - distance, i) for i in devices if i - distance in devices]
    return lax.ppermute(block, axis, route)


def regressors(frames_flat, link_rows, lag_steps, topology):
    samples = frames_flat.shape[0]
    frames = frames_flat.reshape(samples, WIN, GROUPS)
    picker = (
        lax.broadcasted_iota(jnp.int32, (NLAG, WIN), 1) == (WIN - 1 - lag_steps)[:, None]
    ).astype(jnp.bfloat16)
    lagged = jnp.einsum("lw,swg->slg", picker, frames, preferred_element_type=jnp.float32)
    chosen = (link_rows[:, None] == lax.broadcasted_iota(jnp.int32, (samples, GROUPS), 1)).astype(
        jnp.bfloat16
    )
    neighbour = jnp.dot(chosen, topology.astype(jnp.bfloat16), preferred_element_type=jnp.float32)
    design = (lagged * neighbour[:, None, :]).reshape(samples, NLAG * GROUPS).astype(jnp.bfloat16)
    target = jnp.sum(frames[:, WIN - 1, :].astype(jnp.float32) * chosen.astype(jnp.float32), axis=1)
    return (design, target)


def slot_terms(design, target, knot_slot, amount):

    def single(which):
        weight = (knot_slot == which).astype(jnp.bfloat16)
        weighted = design * weight[:, None]
        gram_part = jnp.einsum("sa,sb->ab", weighted, design, preferred_element_type=jnp.float32)
        scaled_target = (target * weight.astype(jnp.float32)).astype(jnp.bfloat16)
        moment_part = jnp.dot(scaled_target, design, preferred_element_type=jnp.float32)
        return jnp.concatenate([gram_part, moment_part[None, :]], 0)

    return lax.map(single, jnp.arange(amount))


def solve_spd(matrix, right_side):
    factor = jnp.linalg.cholesky(matrix)
    return jax.scipy.linalg.cho_solve((factor, True), right_side)


def dense_dot(left_mat, right_mat):
    return jnp.dot(left_mat, right_mat, precision=lax.Precision.HIGHEST)


def body(window, link_ids, knot_ids, lag_steps, topology, smooth):
    n_dp = lax.axis_size("dp")
    n_tm = lax.axis_size("tm")
    device = lax.axis_index("dp") * n_tm + lax.axis_index("tm")
    devices = n_dp * n_tm
    columns = NLAG * GROUPS
    tm_rows, dp_rows, feats = window.shape
    samples = tm_rows * dp_rows
    per_knot = samples // KPD
    design, target = regressors(
        window.reshape(samples, feats), link_ids.reshape(samples), lag_steps, topology
    )
    knot_flat = knot_ids.reshape(samples)
    group_span = KPD * n_tm
    knot_slot = knot_flat // group_span * KPD + knot_flat % KPD
    packed = lax.psum_scatter(
        slot_terms(design, target, knot_slot, KPD * lax.axis_size("dp")),
        "dp",
        scatter_dimension=0,
        tiled=True,
    )
    grams = packed[:, :columns, :] / per_knot
    moments = packed[:, columns, :] / per_knot
    identity = jnp.eye(columns, dtype=jnp.float32)
    penalty_diag = jnp.diag(smooth)
    has_left = (device > 0).astype(jnp.float32)
    has_right = (device < devices - 1).astype(jnp.float32)

    def from_right(solved, stride):
        return from_behind(solved, ("dp", "tm"), -stride)

    def eliminate(system, left_coupling, right_coupling, forcing, left_solved, right_solved):
        left_term = dense_dot(left_coupling, left_solved)
        right_term = dense_dot(right_coupling, right_solved)
        new_system = system - left_term[:, columns : 2 * columns] - right_term[:, :columns]
        new_left = -left_term[:, :columns]
        new_right = -right_term[:, columns : 2 * columns]
        new_forcing = forcing - left_term[:, 2 * columns] - right_term[:, 2 * columns]
        return (new_system, new_left, new_right, new_forcing)

    even_system = grams[0] + RIDGE_TERM * identity + jnp.diag(smooth * (1.0 + has_left))
    even_solved = solve_spd(
        even_system,
        jnp.concatenate([-penalty_diag * has_left, -penalty_diag, moments[0][:, None]], 1),
    )
    next_solved = from_right(even_solved, 1)
    odd_system = grams[1] + RIDGE_TERM * identity + jnp.diag(smooth * (1.0 + has_right))
    system, left_coupling, right_coupling, forcing = eliminate(
        odd_system, -penalty_diag, -penalty_diag * has_right, moments[1], even_solved, next_solved
    )
    height = devices.bit_length() - 1
    for section in range(height):
        stride = 1 << section
        solved = solve_spd(
            system, jnp.concatenate([left_coupling, right_coupling, forcing[:, None]], 1)
        )
        left_in = from_behind(solved, ("dp", "tm"), stride)
        right_in = from_right(solved, stride)
        system, left_coupling, right_coupling, forcing = eliminate(
            system, left_coupling, right_coupling, forcing, left_in, right_in
        )
    solution = solve_spd(system, forcing[:, None])[:, 0]
    prior_odd = from_behind(solution, ("dp", "tm"), 1)
    even_knot = (
        even_solved[:, 2 * columns]
        - dense_dot(even_solved[:, :columns], prior_odd)
        - dense_dot(even_solved[:, columns : 2 * columns], solution)
    )
    return jnp.stack([even_knot, solution]) * jnp.sqrt(jnp.float32(per_knot))


def solution(mesh):
    return jax.shard_map(
        body,
        mesh=mesh,
        in_specs=(P("tm", "dp", None), P("tm", "dp"), P("tm", "dp"), P(), P(), P()),
        out_specs=P(("dp", "tm"), None),
        check_vma=False,
    )
```

profile of v0, /device:TPU:32, one launch (start us, length us, event | category | flops | bytes accessed | tf_op | source)
XLA Modules:
  0.0 1044.4 jit_solution(10829102511843587254)
XLA Ops:
  24.5 51.5 %while.29 = (s32[]{:T(128)}, f32[16,257,256]{2,1,0:T(8,128)}, s32[16]{0:T(128)S(1)}, s32[2048]{0:T(1024)S(1)}, bf16[2048,256]{1,0:T(8,128)(2,1)S(1)}, /*index=5*/f32[2048]{0:T(1024)S(1)}, s32[]{:T(128)}) while((s32[]{:T(128)}, f32[16,257,256]{2,1,0:T(8,128)}, s32[16]{0:T(128)S(1)}, s32[2048]{0:T(1024)S(1)}, bf16[2048,256]{1,0:T(8,128)(2,1)S(1)}, ...), condition=%wide.region_2.3_spmd, body=%wide.region_1.2_spmd.sunk | while | flops 270084352 | bytes 2935389 | solution.py:47
  83.2 47.1 %reduce-scatter.2.cloned.1.call-done = f32[2,257,256]{1,2,0:T(8,128)} async-done(((f32[16,257,256]{1,2,0:T(8,128)}), f32[2,257,256]{1,2,0:T(8,128)}) %reduce-scatter.2.cloned.1.call-update) | async-done | bytes 526352 | tf_op jit(solution)/shard_map/reduce_scatter | solution.py:74
  153.8 11.7 %cholesky.483 = f32[128,128]{1,0:T(8,128)S(1)} custom-call(f32[128,128]{1,0:T(8,128)S(1)} %convolution_subtract_fusion.27), custom_call_target="Cholesky" | custom-call | tf_op jit(solution)/shard_map/jit(cholesky)/cholesky | solution.py:51
  171.7 32.0 %custom-call.39 = f32[2,128,128]{1,2,0:T(8,128)S(1)} custom-call(f32[2,128,128]{2,1,0:T(8,128)S(1)} %get-tuple-element.104), custom_call_target="InvertDiagBlocksLowerTriangular" | custom-call | tf_op jit(solution)/shard_map/jit(_cho_solve)/triangular_solve | solution.py:52
  224.7 11.7 %cholesky.500 = f32[128,128]{1,0:T(8,128)S(1)} custom-call(f32[128,128]{1,0:T(8,128)S(1)} %cholesky.805), custom_call_target="Cholesky" | custom-call | tf_op jit(solution)/shard_map/jit(cholesky)/cholesky | solution.py:51
  246.8 11.7 %cholesky.517 = f32[128,128]{1,0:T(8,128)S(1)} custom-call(f32[128,128]{1,0:T(8,128)S(1)} %convolution_subtract_fusion.26), custom_call_target="Cholesky" | custom-call | tf_op jit(solution)/shard_map/jit(cholesky)/cholesky | solution.py:51
  265.3 19.7 %custom-call.41 = f32[2,128,128]{1,2,0:T(8,128)S(1)} custom-call(f32[2,128,128]{2,1,0:T(8,128)S(1)} %get-tuple-element.105), custom_call_target="InvertDiagBlocksLowerTriangular" | custom-call | tf_op jit(solution)/shard_map/jit(_cho_solve)/triangular_solve | solution.py:52
  313.4 11.7 %cholesky.534 = f32[128,128]{1,0:T(8,128)S(1)} custom-call(f32[128,128]{1,0:T(8,128)S(1)} %cholesky.808), custom_call_target="Cholesky" | custom-call | tf_op jit(solution)/shard_map/jit(cholesky)/cholesky | solution.py:51
  335.4 11.7 %cholesky.551 = f32[128,128]{1,0:T(8,128)S(1)} custom-call(f32[128,128]{1,0:T(8,128)S(1)} %convolution_subtract_fusion.25), custom_call_target="Cholesky" | custom-call | tf_op jit(solution)/shard_map/jit(cholesky)/cholesky | solution.py:51
  354.1 19.7 %custom-call.43 = f32[2,128,128]{1,2,0:T(8,128)S(1)} custom-call(f32[2,128,128]{2,1,0:T(8,128)S(1)} %get-tuple-element.106), custom_call_target="InvertDiagBlocksLowerTriangular" | custom-call | tf_op jit(solution)/shard_map/jit(_cho_solve)/triangular_solve | solution.py:52
  384.8 18.8 %collective-permute-done.4 = f32[256,513]{0,1:T(8,128)} collective-permute-done((f32[256,513]{0,1:T(8,128)S(1)}, f32[256,513]{0,1:T(8,128)}, u32[]{:S(2)}, u32[]{:S(2)}) %collective-permute-start.4) | collective-permute-done | bytes 525344 | tf_op jit(solution)/shard_map/ppermute | solution.py:18
  407.3 11.7 %cholesky.568 = f32[128,128]{1,0:T(8,128)S(1)} custom-call(f32[128,128]{1,0:T(8,128)S(1)} %cholesky.811), custom_call_target="Cholesky" | custom-call | tf_op jit(solution)/shard_map/jit(cholesky)/cholesky | solution.py:51
  429.4 11.7 %cholesky.585 = f32[128,128]{1,0:T(8,128)S(1)} custom-call(f32[128,128]{1,0:T(8,128)S(1)} %convolution_subtract_fusion.24), custom_call_target="Cholesky" | custom-call | tf_op jit(solution)/shard_map/jit(cholesky)/cholesky | solution.py:51
  448.3 19.7 %custom-call.45 = f32[2,128,128]{1,2,0:T(8,128)S(1)} custom-call(f32[2,128,128]{2,1,0:T(8,128)S(1)} %get-tuple-element.107), custom_call_target="InvertDiagBlocksLowerTriangular" | custom-call | tf_op jit(solution)/shard_map/jit(_cho_solve)/triangular_solve | solution.py:52
  490.5 11.7 %cholesky.602 = f32[128,128]{1,0:T(8,128)S(1)} custom-call(f32[128,128]{1,0:T(8,128)S(1)} %cholesky.814), custom_call_target="Cholesky" | custom-call | tf_op jit(solution)/shard_map/jit(cholesky)/cholesky | solution.py:51
  512.6 11.7 %cholesky.619 = f32[128,128]{1,0:T(8,128)S(1)} custom-call(f32[128,128]{1,0:T(8,128)S(1)} %convolution_subtract_fusion.23), custom_call_target="Cholesky" | custom-call | tf_op jit(solution)/shard_map/jit(cholesky)/cholesky | solution.py:51
  531.3 19.7 %custom-call.47 = f32[2,128,128]{1,2,0:T(8,128)S(1)} custom-call(f32[2,128,128]{2,1,0:T(8,128)S(1)} %get-tuple-element.108), custom_call_target="InvertDiagBlocksLowerTriangular" | custom-call | tf_op jit(solution)/shard_map/jit(_cho_solve)/triangular_solve | solution.py:52
  563.0 20.4 %collective-permute-done.8 = f32[256,513]{0,1:T(8,128)} collective-permute-done((f32[256,513]{0,1:T(8,128)S(1)}, f32[256,513]{0,1:T(8,128)}, u32[]{:S(2)}, u32[]{:S(2)}) %collective-permute-start.8) | collective-permute-done | bytes 525344 | tf_op jit(solution)/shard_map/ppermute | solution.py:18
  609.2 11.7 %cholesky.653 = f32[128,128]{1,0:T(8,128)S(1)} custom-call(f32[128,128]{1,0:T(8,128)S(1)} %convolution_subtract_fusion.22), custom_call_target="Cholesky" | custom-call | tf_op jit(solution)/shard_map/jit(cholesky)/cholesky | solution.py:51
  628.0 19.7 %custom-call.49 = f32[2,128,128]{1,2,0:T(8,128)S(1)} custom-call(f32[2,128,128]{2,1,0:T(8,128)S(1)} %get-tuple-element.109), custom_call_target="InvertDiagBlocksLowerTriangular" | custom-call | tf_op jit(solution)/shard_map/jit(_cho_solve)/triangular_solve | solution.py:52
  697.8 11.7 %cholesky.687 = f32[128,128]{1,0:T(8,128)S(1)} custom-call(f32[128,128]{1,0:T(8,128)S(1)} %convolution_subtract_fusion.21), custom_call_target="Cholesky" | custom-call | tf_op jit(solution)/shard_map/jit(cholesky)/cholesky | solution.py:51
  716.5 19.7 %custom-call.51 = f32[2,128,128]{1,2,0:T(8,128)S(1)} custom-call(f32[2,128,128]{2,1,0:T(8,128)S(1)} %get-tuple-element.110), custom_call_target="InvertDiagBlocksLowerTriangular" | custom-call | tf_op jit(solution)/shard_map/jit(_cho_solve)/triangular_solve | solution.py:52
  741.9 34.7 %collective-permute-start.11 = (f32[256,513]{0,1:T(8,128)}, f32[256,513]{0,1:T(8,128)}, u32[]{:S(2)}, u32[]{:S(2)}) collective-permute-start(f32[256,513]{0,1:T(8,128)} %pad_maximum_fusion.13), channel_id=1, source_target_pairs={{0,32},{1,33},{2,34},{3,35},{4,36},{5,37},{6,38},{7,39},{8,40},{9,... | collective-permute-start | bytes 1575944 | tf_op jit(solution)/shard_map/ppermute | solution.py:18
  780.4 11.7 %cholesky.704 = f32[128,128]{1,0:T(8,128)S(1)} custom-call(f32[128,128]{1,0:T(8,128)S(1)} %cholesky.823), custom_call_target="Cholesky" | custom-call | tf_op jit(solution)/shard_map/jit(cholesky)/cholesky | solution.py:51
  802.5 11.7 %cholesky.721 = f32[128,128]{1,0:T(8,128)S(1)} custom-call(f32[128,128]{1,0:T(8,128)S(1)} %convolution_subtract_fusion.20), custom_call_target="Cholesky" | custom-call | tf_op jit(solution)/shard_map/jit(cholesky)/cholesky | solution.py:51
  820.9 20.3 %custom-call.53 = f32[2,128,128]{1,2,0:T(8,128)} custom-call(f32[2,128,128]{2,1,0:T(8,128)S(1)} %get-tuple-element.111), custom_call_target="InvertDiagBlocksLowerTriangular" | custom-call | tf_op jit(solution)/shard_map/jit(_cho_solve)/triangular_solve | solution.py:52
  848.7 13.3 %collective-permute-start.13 = (f32[256,513]{0,1:T(8,128)S(1)}, f32[256,513]{0,1:T(8,128)}, u32[]{:S(2)}, u32[]{:S(2)}) collective-permute-start(f32[256,513]{0,1:T(8,128)S(1)} %pad_maximum_fusion.15), channel_id=1, source_target_pairs={{0,64},{1,65},{2,66},{3,67},{4,68},{5,69},{6,70},{7,71},{8,72},{9,... | collective-permute-start | bytes 1575944 | tf_op jit(solution)/shard_map/ppermute | solution.py:18
  894.1 11.7 %cholesky.755 = f32[128,128]{1,0:T(8,128)S(1)} custom-call(f32[128,128]{1,0:T(8,128)S(1)} %convolution_subtract_fusion.19), custom_call_target="Cholesky" | custom-call | tf_op jit(solution)/shard_map/jit(cholesky)/cholesky | solution.py:51
  912.8 19.7 %custom-call.55 = f32[2,128,128]{1,2,0:T(8,128)S(1)} custom-call(f32[2,128,128]{2,1,0:T(8,128)S(1)} %get-tuple-element.112), custom_call_target="InvertDiagBlocksLowerTriangular" | custom-call | tf_op jit(solution)/shard_map/jit(_cho_solve)/triangular_solve | solution.py:52
  936.1 13.8 %collective-permute-start.15 = (f32[256,513]{0,1:T(8,128)S(1)}, f32[256,513]{0,1:T(8,128)S(1)}, u32[]{:S(2)}, u32[]{:S(2)}) collective-permute-start(f32[256,513]{0,1:T(8,128)S(1)} %pad_maximum_fusion.17), channel_id=1, source_target_pairs={{0,128},{1,129},{2,130},{3,131},{4,132},{5,133},{6,134},{7,135},{8... | collective-permute-start | bytes 1575944 | tf_op jit(solution)/shard_map/ppermute | solution.py:18
  988.5 11.7 %cholesky.789 = f32[128,128]{1,0:T(8,128)S(1)} custom-call(f32[128,128]{1,0:T(8,128)S(1)} %convolution_subtract_fusion.18), custom_call_target="Cholesky" | custom-call | tf_op jit(solution)/shard_map/jit(cholesky)/cholesky | solution.py:51
  1007.7 19.7 %custom-call.20 = f32[2,128,128]{1,2,0:T(8,128)S(1)} custom-call(f32[2,128,128]{2,1,0:T(8,128)S(1)} %get-tuple-element.55), custom_call_target="InvertDiagBlocksLowerTriangular" | custom-call | tf_op jit(solution)/shard_map/jit(_cho_solve)/triangular_solve | solution.py:52
  (504 shorter events, 522.3 us)
Async XLA Ops:
  6.5 123.8 %reduce-scatter.2.cloned.1.call-start = ((), (), s32[]{:S(2)}) async-start(), calls=%async_computation.1 | async-start | bytes 7077888 | tf_op jit(solution)/shard_map/reduce_scatter | solution.py:74
  12.7 8.5 copy-start.5
  12.7 8.6 copy-start.7
  12.7 8.6 copy-start.3
  21.9 2.5 copy-start.6
  82.5 0.7 copy-start.4
  208.5 15.3 %collective-permute-start = (f32[256,513]{0,1:T(8,128)S(1)}, f32[256,513]{0,1:T(8,128)S(1)}, u32[]{:S(2)}, u32[]{:S(2)}) collective-permute-start(f32[256,513]{0,1:T(8,128)S(1)} %pad_maximum_fusion), channel_id=1, source_target_pairs={{1,0},{2,1},{3,2},{4,3},{5,4},{6,5},{7,6},{8,7},{9,8},{10,9},{11,1... | collective-permute-start | bytes 1575944 | tf_op jit(solution)/shard_map/ppermute | solution.py:18
  288.6 16.4 %collective-permute-start.2 = (f32[256,513]{0,1:T(8,128)S(1)}, f32[256,513]{0,1:T(8,128)}, u32[]{:S(2)}, u32[]{:S(2)}) collective-permute-start(f32[256,513]{0,1:T(8,128)S(1)} %pad_maximum_fusion.3), channel_id=1, source_target_pairs={{1,0},{2,1},{3,2},{4,3},{5,4},{6,5},{7,6},{8,7},{9,8},{10,9},{11,1... | collective-permute-start | bytes 1575944 | tf_op jit(solution)/shard_map/ppermute | solution.py:18
  295.1 16.3 %collective-permute-start.1 = (f32[256,513]{0,1:T(8,128)S(1)}, f32[256,513]{0,1:T(8,128)}, u32[]{:S(2)}, u32[]{:S(2)}) collective-permute-start(f32[256,513]{0,1:T(8,128)S(1)} %pad_maximum_fusion.3), channel_id=1, source_target_pairs={{0,1},{1,2},{2,3},{3,4},{4,5},{5,6},{6,7},{7,8},{8,9},{9,10},{10,1... | collective-permute-start | bytes 1575944 | tf_op jit(solution)/shard_map/ppermute | solution.py:18
  377.5 26.2 %collective-permute-start.4 = (f32[256,513]{0,1:T(8,128)S(1)}, f32[256,513]{0,1:T(8,128)}, u32[]{:S(2)}, u32[]{:S(2)}) collective-permute-start(f32[256,513]{0,1:T(8,128)S(1)} %pad_maximum_fusion.5), channel_id=1, source_target_pairs={{2,0},{3,1},{4,2},{5,3},{6,4},{7,5},{8,6},{9,7},{10,8},{11,9},{12,... | collective-permute-start | bytes 1575944 | tf_op jit(solution)/shard_map/ppermute | solution.py:18
  379.4 25.9 %collective-permute-start.3 = (f32[256,513]{0,1:T(8,128)S(1)}, f32[256,513]{0,1:T(8,128)}, u32[]{:S(2)}, u32[]{:S(2)}) collective-permute-start(f32[256,513]{0,1:T(8,128)S(1)} %pad_maximum_fusion.5), channel_id=1, source_target_pairs={{0,2},{1,3},{2,4},{3,5},{4,6},{5,7},{6,8},{7,9},{8,10},{9,11},{10,... | collective-permute-start | bytes 1575944 | tf_op jit(solution)/shard_map/ppermute | solution.py:18
  471.7 13.1 %collective-permute-start.6 = (f32[256,513]{0,1:T(8,128)S(1)}, f32[256,513]{0,1:T(8,128)}, u32[]{:S(2)}, u32[]{:S(2)}) collective-permute-start(f32[256,513]{0,1:T(8,128)S(1)} %pad_maximum_fusion.7), channel_id=1, source_target_pairs={{4,0},{5,1},{6,2},{7,3},{8,4},{9,5},{10,6},{11,7},{12,8},{13,9},{1... | collective-permute-start | bytes 1575944 | tf_op jit(solution)/shard_map/ppermute | solution.py:18
  473.6 15.0 %collective-permute-start.5 = (f32[256,513]{0,1:T(8,128)S(1)}, f32[256,513]{0,1:T(8,128)}, u32[]{:S(2)}, u32[]{:S(2)}) collective-permute-start(f32[256,513]{0,1:T(8,128)S(1)} %pad_maximum_fusion.7), channel_id=1, source_target_pairs={{0,4},{1,5},{2,6},{3,7},{4,8},{5,9},{6,10},{7,11},{8,12},{9,13},{1... | collective-permute-start | bytes 1575944 | tf_op jit(solution)/shard_map/ppermute | solution.py:18
  554.6 28.8 %collective-permute-start.8 = (f32[256,513]{0,1:T(8,128)S(1)}, f32[256,513]{0,1:T(8,128)}, u32[]{:S(2)}, u32[]{:S(2)}) collective-permute-start(f32[256,513]{0,1:T(8,128)S(1)} %pad_maximum_fusion.9), channel_id=1, source_target_pairs={{8,0},{9,1},{10,2},{11,3},{12,4},{13,5},{14,6},{15,7},{16,8},{17,9... | collective-permute-start | bytes 1575944 | tf_op jit(solution)/shard_map/ppermute | solution.py:18
  555.9 29.2 %collective-permute-start.7 = (f32[256,513]{0,1:T(8,128)S(1)}, f32[256,513]{0,1:T(8,128)}, u32[]{:S(2)}, u32[]{:S(2)}) collective-permute-start(f32[256,513]{0,1:T(8,128)S(1)} %pad_maximum_fusion.9), channel_id=1, source_target_pairs={{0,8},{1,9},{2,10},{3,11},{4,12},{5,13},{6,14},{7,15},{8,16},{9,17... | collective-permute-start | bytes 1575944 | tf_op jit(solution)/shard_map/ppermute | solution.py:18
  651.4 19.8 %collective-permute-start.10 = (f32[256,513]{0,1:T(8,128)S(1)}, f32[256,513]{0,1:T(8,128)}, u32[]{:S(2)}, u32[]{:S(2)}) collective-permute-start(f32[256,513]{0,1:T(8,128)S(1)} %pad_maximum_fusion.11), channel_id=1, source_target_pairs={{16,0},{17,1},{18,2},{19,3},{20,4},{21,5},{22,6},{23,7},{24,8},{25... | collective-permute-start | bytes 1575944 | tf_op jit(solution)/shard_map/ppermute | solution.py:18
  652.7 21.1 %collective-permute-start.9 = (f32[256,513]{0,1:T(8,128)S(1)}, f32[256,513]{0,1:T(8,128)}, u32[]{:S(2)}, u32[]{:S(2)}) collective-permute-start(f32[256,513]{0,1:T(8,128)S(1)} %pad_maximum_fusion.11), channel_id=1, source_target_pairs={{0,16},{1,17},{2,18},{3,19},{4,20},{5,21},{6,22},{7,23},{8,24},{9,... | collective-permute-start | bytes 1575944 | tf_op jit(solution)/shard_map/ppermute | solution.py:18
  740.6 36.0 %collective-permute-start.12 = (f32[256,513]{0,1:T(8,128)}, f32[256,513]{0,1:T(8,128)S(1)}, u32[]{:S(2)}, u32[]{:S(2)}) collective-permute-start(f32[256,513]{0,1:T(8,128)} %pad_maximum_fusion.13), channel_id=1, source_target_pairs={{32,0},{33,1},{34,2},{35,3},{36,4},{37,5},{38,6},{39,7},{40,8},{41... | collective-permute-start | bytes 1575944 | tf_op jit(solution)/shard_map/ppermute | solution.py:18
  741.9 35.7 %collective-permute-start.11 = (f32[256,513]{0,1:T(8,128)}, f32[256,513]{0,1:T(8,128)}, u32[]{:S(2)}, u32[]{:S(2)}) collective-permute-start(f32[256,513]{0,1:T(8,128)} %pad_maximum_fusion.13), channel_id=1, source_target_pairs={{0,32},{1,33},{2,34},{3,35},{4,36},{5,37},{6,38},{7,39},{8,40},{9,... | collective-permute-start | bytes 1575944 | tf_op jit(solution)/shard_map/ppermute | solution.py:18
  779.3 63.9 %copy-start = (f32[256,513]{0,1:T(8,128)}, f32[256,513]{0,1:T(8,128)S(1)}, u32[]{:S(2)}) copy-start(f32[256,513]{0,1:T(8,128)S(1)} %fusion.166) | copy-start | bytes 1575940
  780.2 61.0 %copy-start.1 = (f32[256,256]{0,1:T(8,128)S(1)}, f32[256,256]{0,1:T(8,128)}, u32[]{:S(2)}) copy-start(f32[256,256]{0,1:T(8,128)} %get-tuple-element.272) | copy-start | bytes 786436
  841.2 5.6 copy-start.2
  847.4 20.9 %collective-permute-start.14 = (f32[256,513]{0,1:T(8,128)S(1)}, f32[256,513]{0,1:T(8,128)}, u32[]{:S(2)}, u32[]{:S(2)}) collective-permute-start(f32[256,513]{0,1:T(8,128)S(1)} %pad_maximum_fusion.15), channel_id=1, source_target_pairs={{64,0},{65,1},{66,2},{67,3},{68,4},{69,5},{70,6},{71,7},{72,8},{73... | collective-permute-start | bytes 1575944 | tf_op jit(solution)/shard_map/ppermute | solution.py:18
  848.7 21.3 %collective-permute-start.13 = (f32[256,513]{0,1:T(8,128)S(1)}, f32[256,513]{0,1:T(8,128)}, u32[]{:S(2)}, u32[]{:S(2)}) collective-permute-start(f32[256,513]{0,1:T(8,128)S(1)} %pad_maximum_fusion.15), channel_id=1, source_target_pairs={{0,64},{1,65},{2,66},{3,67},{4,68},{5,69},{6,70},{7,71},{8,72},{9,... | collective-permute-start | bytes 1575944 | tf_op jit(solution)/shard_map/ppermute | solution.py:18
  936.1 23.7 %collective-permute-start.15 = (f32[256,513]{0,1:T(8,128)S(1)}, f32[256,513]{0,1:T(8,128)S(1)}, u32[]{:S(2)}, u32[]{:S(2)}) collective-permute-start(f32[256,513]{0,1:T(8,128)S(1)} %pad_maximum_fusion.17), channel_id=1, source_target_pairs={{0,128},{1,129},{2,130},{3,131},{4,132},{5,133},{6,134},{7,135},{8... | collective-permute-start | bytes 1575944 | tf_op jit(solution)/shard_map/ppermute | solution.py:18
  949.9 15.6 %collective-permute-start.16 = (f32[256,513]{0,1:T(8,128)S(1)}, f32[256,513]{0,1:T(8,128)S(1)}, u32[]{:S(2)}, u32[]{:S(2)}) collective-permute-start(f32[256,513]{0,1:T(8,128)S(1)} %pad_maximum_fusion.17), channel_id=1, source_target_pairs={{128,0},{129,1},{130,2},{131,3},{132,4},{133,5},{134,6},{135,7},{1... | collective-permute-start | bytes 1575944 | tf_op jit(solution)/shard_map/ppermute | solution.py:18
  1028.9 7.6 collective-permute-start.17
Sparse Core Ops, SparseCore 0:
  82.7 47.6 reduce-scatter.1
where the time goes:
time: 1050 us; the launch traced here: 1040 us
  other arithmetic  588 us (56%)
  waiting for transfers between devices  155 us (15%)
  starting transfers between devices  113 us (11%)
  matrix products  84 us (8%)
  local copies, waits for them, and re-layouts  73.1 us (7%)
  between operations  28 us (3%)
    another operation x69, other arithmetic, solve_spd(): factor = jnp.linalg.cholesky(matrix)  346 us
    another operation x32, other arithmetic, solve_spd(): return jax.scipy.linalg.cho_solve((factor, True), right_side)  211 us
    ppermute x18, starting transfers between devices, from_behind(): return lax.ppermute(block, axis, route)  113 us
    ppermute x18, waiting for transfers between devices, from_behind(): return lax.ppermute(block, axis, route)  108 us
    reduce_scatter x1, waiting for transfers between devices, body(): lax.psum_scatter(slot_terms(design, target, knot_slot, KPD * lax.axis_siz...  47.1 us
    another operation x65, local copies, waits for them, and re-layouts, solve_spd(): return jax.scipy.linalg.cho_solve((factor, True), right_side)  35.7 us
    another operation x60, matrix products, solve_spd(): return jax.scipy.linalg.cho_solve((factor, True), right_side)  35.3 us
    dot_general x20, matrix products, dense_dot(): return jnp.dot(left_mat, right_mat, precision=lax.Precision.HIGHEST)  25.2 us
  transfers between devices with their start and end apart: 19, of which 15 were waited for; matrix products, arithmetic and copies ran while one was open for 1% of the time, Pallas kernels for 0%

commit v1 on v0

--- a/solution.py
+++ b/solution.py
@@ -47,9 +47,47 @@
     return lax.map(single, jnp.arange(amount))
 
 
-def solve_spd(matrix, right_side):
+def cholesky_solve(matrix, right_side):
     factor = jnp.linalg.cholesky(matrix)
     return jax.scipy.linalg.cho_solve((factor, True), right_side)
+
+
+NS_TOL2 = 1e-6
+NS_MAX_STEPS = 30
+
+
+def solve_spd(matrix, right_side):
+    size = matrix.shape[0]
+    identity = jnp.eye(size, dtype=jnp.float32)
+    inv_diag = 1.0 / jnp.diagonal(matrix)
+    rows = jnp.sum(jnp.abs(matrix * inv_diag[:, None]), axis=1)
+    upper = jnp.max(rows)
+    lower = jnp.maximum(jnp.min(2.0 - rows), 0.0)
+    start = jnp.diag(inv_diag * (2.0 / (upper + lower)))
+
+    def residual(inverse):
+        gap = identity - dense_dot(inverse, matrix)
+        return gap, jnp.sum(gap * gap)
+
+    def going(state):
+        _, _, norm2, step = state
+        return (step < NS_MAX_STEPS) & (norm2 > NS_TOL2) & jnp.isfinite(norm2)
+
+    def refine(state):
+        inverse, gap, _, step = state
+        inverse = inverse + dense_dot(gap, inverse)
+        gap, norm2 = residual(inverse)
+        return (inverse, gap, norm2, step + 1)
+
+    gap0, norm0 = residual(start)
+    inverse, gap, norm2, _ = lax.while_loop(going, refine, (start, gap0, norm0, 0))
+    inverse = inverse + dense_dot(gap, inverse)
+    quick = dense_dot(inverse, right_side)
+    return lax.cond(
+        norm2 <= NS_TOL2,
+        lambda: quick,
+        lambda: cholesky_solve(matrix, right_side),
+    )
 
 
 def dense_dot(left_mat, right_mat):

time: 1050 us -> 637 us (0.61)
  other arithmetic: 588 us -> 47.1 us
  loops' own time: 3.47 us -> 103 us
  matrix products: 84 us -> 124 us
  starting transfers between devices: 113 us -> 87.6 us
    another operation x102 -> x0, other arithmetic: 557 us -> none  [the longest x69 346 us: solve_spd(): factor = jnp.linalg.cholesky(matrix)]
    another operation x10 -> x20, loops' own time: 3.08 us -> 103 us  [the longest x10 64.9 us: solve_spd(): lax.while_loop(going, refine, (start, gap0, norm0, 0))]
    dot_general x20 -> x132, matrix products: 25.2 us -> 105 us  [dense_dot(): return jnp.dot(left_mat, right_mat, precision=lax.Precision.HIGHEST)]
    another operation x100 -> x2, local copies, waits for them, and re-layouts: 40.5 us -> 0.14 us  [body(): moments[0][:, None]]
    another operation x80 -> x0, matrix products: 40.1 us -> none  [the longest x60 35.3 us: solve_spd(): return jax.scipy.linalg.cho_solve((factor, True), right_side)]
    ppermute x18, starting transfers between devices: 113 us -> 87.6 us  [from_behind(): return lax.ppermute(block, axis, route)]
    gather x0 -> x10, local copies, waits for them, and re-layouts: none -> 23.4 us  [solve_spd(): inv_diag = 1.0 / jnp.diagonal(matrix)]
    ppermute x18, waiting for transfers between devices: 108 us -> 123 us  [from_behind(): return lax.ppermute(block, axis, route)]
  transfers between devices with their start and end apart: 19 -> 19, of which waited for: 15 -> 19; matrix products, arithmetic and copies ran while one was open for 1% -> 1% of each run, Pallas kernels for 0% -> 0%
where the time goes in v1:
time: 637 us; the launch traced here: 627 us
  waiting for transfers between devices  165 us (26%)
  matrix products  124 us (19%)
  loops' own time  103 us (16%)
  starting transfers between devices  87.6 us (14%)
  local copies, waits for them, and re-layouts  64.8 us (10%)
  other arithmetic  47.1 us (7%)
  between operations  34.3 us (5%)
    ppermute x18, waiting for transfers between devices, from_behind(): return lax.ppermute(block, axis, route)  123 us
    dot_general x132, matrix products, dense_dot(): return jnp.dot(left_mat, right_mat, precision=lax.Precision.HIGHEST)  105 us
    ppermute x18, starting transfers between devices, from_behind(): return lax.ppermute(block, axis, route)  87.6 us
    another operation x10, loops' own time, solve_spd(): lax.while_loop(going, refine, (start, gap0, norm0, 0))  64.9 us
    reduce_scatter x1, waiting for transfers between devices, body(): lax.psum_scatter(slot_terms(design, target, knot_slot, KPD * lax.axis_siz...  42.8 us
    another operation x10, loops' own time, solve_spd(): lax.cond(norm2 <= NS_TOL2, lambda: quick, lambda: cholesky_solve(matrix,...  38.2 us
    gather x10, local copies, waits for them, and re-layouts, solve_spd(): inv_diag = 1.0 / jnp.diagonal(matrix)  23.4 us
    cond x10, local copies, waits for them, and re-layouts  14.3 us
  transfers between devices with their start and end apart: 19, of which 19 were waited for; matrix products, arithmetic and copies ran while one was open for 1% of the time, Pallas kernels for 0%

profile of v1, /device:TPU:32, one launch (start us, length us, event | category | flops | bytes accessed | tf_op | source)
XLA Modules:
  0.0 626.9 jit_solution(9638049539804054367)
XLA Ops:
  6.5 6.2 reshape_reshape.3
  12.7 5.9 copy.64
  26.5 49.4 %while.189 = (s32[]{:T(128)}, f32[16,257,256]{2,1,0:T(8,128)}, s32[16]{0:T(128)S(1)}, s32[2048]{0:T(1024)S(1)}, bf16[2048,256]{1,0:T(8,128)(2,1)S(1)}, /*index=5*/f32[2048]{0:T(1024)S(1)}, s32[]{:T(128)}) while((s32[]{:T(128)}, f32[16,257,256]{2,1,0:T(8,128)}, s32[16]{0:T(128)S(1)}, s32[2048]{0:T(1024)S(1)}, bf16[2048,256]{1,0:T(8,128)(2,1)S(1)}, ...), condition=%wide.region_2.3_spmd, body=%wide.region_1.2_spmd.sunk | while | flops 270084352 | bytes 2935389 | solution.py:47
  76.7 42.8 %reduce-scatter.2.cloned.1.call-done = f32[2,257,256]{2,1,0:T(8,128)} async-done(((f32[16,257,256]{2,1,0:T(8,128)}), f32[2,257,256]{2,1,0:T(8,128)}) %reduce-scatter.2.cloned.1.call-update) | async-done | bytes 526352 | tf_op jit(solution)/shard_map/reduce_scatter | solution.py:112
  142.7 7.6 %collective-permute-done = f32[256,513]{0,1:T(8,128)} collective-permute-done((f32[256,513]{0,1:T(8,128)S(1)}, f32[256,513]{0,1:T(8,128)}, u32[]{:S(2)}, u32[]{:S(2)}) %collective-permute-start) | collective-permute-done | bytes 525344 | tf_op jit(solution)/shard_map/ppermute | solution.py:18
  165.2 6.2 conditional.11
  179.9 6.6 %collective-permute-done.1 = f32[256,513]{0,1:T(8,128)S(1)} collective-permute-done((f32[256,513]{0,1:T(8,128)}, f32[256,513]{0,1:T(8,128)S(1)}, u32[]{:S(2)}, u32[]{:S(2)}) %collective-permute-start.1) | collective-permute-done | bytes 525344 | tf_op jit(solution)/shard_map/ppermute | solution.py:18
  195.5 6.7 %while.192 = (f32[256,256]{1,0:T(8,128)S(1)}, f32[256,256]{1,0:T(8,128)S(1)}, f32[]{:T(128)}, s32[]{:T(128)}, f32[256,256]{1,0:T(8,128)S(1)}, /*index=5*/s32[]{:T(128)}) while((f32[256,256]{1,0:T(8,128)S(1)}, f32[256,256]{1,0:T(8,128)S(1)}, f32[]{:T(128)}, s32[]{:T(128)}, f32[256,256]{1,0:T(8,128)S(1)}, ...), condition=%wide.region_32.35_spmd.clone, body=%wide.region_30.34_spmd.clone.sunk | while | flops 403046400 | bytes 2097245 | solution.py:83
  205.4 5.9 conditional.12
  211.3 5.6 collective-permute-start.3
  219.6 15.6 %collective-permute-done.3 = f32[256,513]{0,1:T(8,128)S(1)} collective-permute-done((f32[256,513]{0,1:T(8,128)}, f32[256,513]{0,1:T(8,128)S(1)}, u32[]{:S(2)}, u32[]{:S(2)}) %collective-permute-start.3) | collective-permute-done | bytes 525344 | tf_op jit(solution)/shard_map/ppermute | solution.py:18
  244.2 6.8 %while.193 = (f32[256,256]{1,0:T(8,128)S(1)}, f32[256,256]{1,0:T(8,128)S(1)}, f32[]{:T(128)}, s32[]{:T(128)}, f32[256,256]{1,0:T(8,128)S(1)}, /*index=5*/s32[]{:T(128)}) while((f32[256,256]{1,0:T(8,128)S(1)}, f32[256,256]{1,0:T(8,128)S(1)}, f32[]{:T(128)}, s32[]{:T(128)}, f32[256,256]{1,0:T(8,128)S(1)}, ...), condition=%wide.region_41.44_spmd.clone, body=%wide.region_39.43_spmd.clone.sunk | while | flops 403046400 | bytes 2097245 | solution.py:83
  254.3 6.1 conditional.13
  263.9 12.3 %collective-permute-start.6 = (f32[256,513]{0,1:T(8,128)}, f32[256,513]{0,1:T(8,128)}, u32[]{:S(2)}, u32[]{:S(2)}) collective-permute-start(f32[256,513]{0,1:T(8,128)} %get-tuple-element.2181), channel_id=1, source_target_pairs={{4,0},{5,1},{6,2},{7,3},{8,4},{9,5},{10,6},{11,7},{12,8},{13,9},{1... | collective-permute-start | bytes 1575944 | tf_op jit(solution)/shard_map/ppermute | solution.py:18
  276.3 7.6 %collective-permute-done.5 = f32[256,513]{0,1:T(8,128)S(1)} collective-permute-done((f32[256,513]{0,1:T(8,128)}, f32[256,513]{0,1:T(8,128)S(1)}, u32[]{:S(2)}, u32[]{:S(2)}) %collective-permute-start.5) | collective-permute-done | bytes 525344 | tf_op jit(solution)/shard_map/ppermute | solution.py:18
  292.8 14.8 %while.194 = (f32[256,256]{1,0:T(8,128)S(1)}, f32[256,256]{1,0:T(8,128)S(1)}, f32[]{:T(128)}, s32[]{:T(128)}, f32[256,256]{1,0:T(8,128)S(1)}, /*index=5*/s32[]{:T(128)}) while((f32[256,256]{1,0:T(8,128)S(1)}, f32[256,256]{1,0:T(8,128)S(1)}, f32[]{:T(128)}, s32[]{:T(128)}, f32[256,256]{1,0:T(8,128)S(1)}, ...), condition=%wide.region_50.53_spmd.clone, body=%wide.region_48.52_spmd.clone.sunk | while | flops 403046400 | bytes 2097245 | solution.py:83
  310.9 5.9 conditional.14
  319.5 19.6 %collective-permute-done.7 = f32[256,513]{0,1:T(8,128)S(1)} collective-permute-done((f32[256,513]{0,1:T(8,128)}, f32[256,513]{0,1:T(8,128)S(1)}, u32[]{:S(2)}, u32[]{:S(2)}) %collective-permute-start.7) | collective-permute-done | bytes 525344 | tf_op jit(solution)/shard_map/ppermute | solution.py:18
  347.9 17.6 %while.195 = (f32[256,256]{1,0:T(8,128)S(1)}, f32[256,256]{1,0:T(8,128)S(1)}, f32[]{:T(128)}, s32[]{:T(128)}, f32[256,256]{1,0:T(8,128)S(1)}, /*index=5*/s32[]{:T(128)}) while((f32[256,256]{1,0:T(8,128)S(1)}, f32[256,256]{1,0:T(8,128)S(1)}, f32[]{:T(128)}, s32[]{:T(128)}, f32[256,256]{1,0:T(8,128)S(1)}, ...), condition=%wide.region_59.62_spmd.clone, body=%wide.region_57.61_spmd.clone.sunk | while | flops 403046400 | bytes 2097245 | solution.py:83
  368.7 6.2 conditional.15
  380.4 15.2 %collective-permute-done.9 = f32[256,513]{0,1:T(8,128)S(1)} collective-permute-done((f32[256,513]{0,1:T(8,128)}, f32[256,513]{0,1:T(8,128)S(1)}, u32[]{:S(2)}, u32[]{:S(2)}) %collective-permute-start.9) | collective-permute-done | bytes 525344 | tf_op jit(solution)/shard_map/ppermute | solution.py:18
  409.5 17.8 %while.196 = (f32[256,256]{1,0:T(8,128)S(1)}, f32[256,256]{1,0:T(8,128)S(1)}, f32[]{:T(128)}, s32[]{:T(128)}, f32[256,256]{1,0:T(8,128)S(1)}, /*index=5*/s32[]{:T(128)}) while((f32[256,256]{1,0:T(8,128)S(1)}, f32[256,256]{1,0:T(8,128)S(1)}, f32[]{:T(128)}, s32[]{:T(128)}, f32[256,256]{1,0:T(8,128)S(1)}, ...), condition=%wide.region_68.71_spmd.clone, body=%wide.region_66.70_spmd.clone.sunk | while | flops 403046400 | bytes 2097245 | solution.py:83
  430.7 5.9 conditional.16
  436.6 26.0 %collective-permute-start.11 = (f32[256,513]{0,1:T(8,128)}, f32[256,513]{0,1:T(8,128)S(1)}, u32[]{:S(2)}, u32[]{:S(2)}) collective-permute-start(f32[256,513]{0,1:T(8,128)} %get-tuple-element.2184), channel_id=1, source_target_pairs={{0,32},{1,33},{2,34},{3,35},{4,36},{5,37},{6,38},{7,39},{8,40},{9,... | collective-permute-start | bytes 1575944 | tf_op jit(solution)/shard_map/ppermute | solution.py:18
  465.0 9.1 %collective-permute-done.12 = f32[256,513]{0,1:T(8,128)} collective-permute-done((f32[256,513]{0,1:T(8,128)}, f32[256,513]{0,1:T(8,128)}, u32[]{:S(2)}, u32[]{:S(2)}) %collective-permute-start.12) | collective-permute-done | bytes 525344 | tf_op jit(solution)/shard_map/ppermute | solution.py:18
  481.7 17.5 %while.197 = (f32[256,256]{1,0:T(8,128)S(1)}, f32[256,256]{1,0:T(8,128)S(1)}, f32[]{:T(128)}, s32[]{:T(128)}, f32[256,256]{1,0:T(8,128)S(1)}, /*index=5*/s32[]{:T(128)}) while((f32[256,256]{1,0:T(8,128)S(1)}, f32[256,256]{1,0:T(8,128)S(1)}, f32[]{:T(128)}, s32[]{:T(128)}, f32[256,256]{1,0:T(8,128)S(1)}, ...), condition=%wide.region_77.80_spmd.clone, body=%wide.region_75.79_spmd.clone.sunk | while | flops 403046400 | bytes 2097245 | solution.py:83
  502.6 6.2 conditional.17
  508.7 6.2 collective-permute-start.13
  516.2 9.5 %collective-permute-done.13 = f32[256,513]{0,1:T(8,128)S(1)} collective-permute-done((f32[256,513]{0,1:T(8,128)}, f32[256,513]{0,1:T(8,128)S(1)}, u32[]{:S(2)}, u32[]{:S(2)}) %collective-permute-start.13) | collective-permute-done | bytes 525344 | tf_op jit(solution)/shard_map/ppermute | solution.py:18
  539.3 17.5 %while.198 = (f32[256,256]{1,0:T(8,128)S(1)}, f32[256,256]{1,0:T(8,128)S(1)}, f32[]{:T(128)}, s32[]{:T(128)}, f32[256,256]{1,0:T(8,128)S(1)}, /*index=5*/s32[]{:T(128)}) while((f32[256,256]{1,0:T(8,128)S(1)}, f32[256,256]{1,0:T(8,128)S(1)}, f32[]{:T(128)}, s32[]{:T(128)}, f32[256,256]{1,0:T(8,128)S(1)}, ...), condition=%wide.region_86.89_spmd.clone, body=%wide.region_84.88_spmd.clone.sunk | while | flops 403046400 | bytes 2097245 | solution.py:83
  569.5 9.6 %collective-permute-done.15 = f32[256,513]{0,1:T(8,128)S(1)} collective-permute-done((f32[256,513]{0,1:T(8,128)S(1)}, f32[256,513]{0,1:T(8,128)S(1)}, u32[]{:S(2)}, u32[]{:S(2)}) %collective-permute-start.15) | collective-permute-done | bytes 525344 | tf_op jit(solution)/shard_map/ppermute | solution.py:18
  592.4 16.3 %while.199 = (f32[256,256]{1,0:T(8,128)S(1)}, f32[256,256]{1,0:T(8,128)S(1)}, f32[]{:T(128)}, s32[]{:T(128)}, f32[256,256]{1,0:T(8,128)S(1)}, /*index=5*/s32[]{:T(128)}) while((f32[256,256]{1,0:T(8,128)S(1)}, f32[256,256]{1,0:T(8,128)S(1)}, f32[]{:T(128)}, s32[]{:T(128)}, f32[256,256]{1,0:T(8,128)S(1)}, ...), condition=%wide.region_95.98_spmd.clone, body=%wide.region_93.97_spmd.clone.sunk | while | flops 403046400 | bytes 2097245 | solution.py:83
  (465 shorter events, 301.7 us)
Async XLA Ops:
  6.5 113.0 %reduce-scatter.2.cloned.1.call-start = ((), (), s32[]{:S(2)}) async-start(), calls=%async_computation.1 | async-start | bytes 4866048 | tf_op jit(solution)/shard_map/reduce_scatter | solution.py:112
  12.7 9.3 %copy-start.8 = (s32[32,64]{1,0:T(8,128)S(1)}, s32[32,64]{1,0:T(8,128)}, u32[]{:S(2)}) copy-start(s32[32,64]{1,0:T(8,128)} %param.52) | copy-start | bytes 24580
  12.7 9.4 %copy-start.10 = (s32[4]{0:T(128)S(1)}, s32[4]{0:T(128)}, u32[]{:S(2)}) copy-start(s32[4]{0:T(128)} %param.54) | copy-start | bytes 52
  12.7 9.4 %copy-start.6 = (s32[64,64]{1,0:T(8,128)S(1)}, s32[64,64]{1,0:T(8,128)}, u32[]{:S(2)}) copy-start(s32[64,64]{1,0:T(8,128)} %param.55) | copy-start | bytes 49156
  22.7 3.8 copy-start.9
  76.0 0.7 copy-start.7
  137.2 13.0 %collective-permute-start = (f32[256,513]{0,1:T(8,128)S(1)}, f32[256,513]{0,1:T(8,128)}, u32[]{:S(2)}, u32[]{:S(2)}) collective-permute-start(f32[256,513]{0,1:T(8,128)S(1)} %get-tuple-element.2178), channel_id=1, source_target_pairs={{1,0},{2,1},{3,2},{4,3},{5,4},{6,5},{7,6},{8,7},{9,8},{10,9},{11,1... | collective-permute-start | bytes 1575944 | tf_op jit(solution)/shard_map/ppermute | solution.py:18
  171.4 15.2 %collective-permute-start.1 = (f32[256,513]{0,1:T(8,128)}, f32[256,513]{0,1:T(8,128)S(1)}, u32[]{:S(2)}, u32[]{:S(2)}) collective-permute-start(f32[256,513]{0,1:T(8,128)} %get-tuple-element.2179), channel_id=1, source_target_pairs={{0,1},{1,2},{2,3},{3,4},{4,5},{5,6},{6,7},{7,8},{8,9},{9,10},{10,1... | collective-permute-start | bytes 1575944 | tf_op jit(solution)/shard_map/ppermute | solution.py:18
  174.8 13.1 %collective-permute-start.2 = (f32[256,513]{0,1:T(8,128)}, f32[256,513]{0,1:T(8,128)}, u32[]{:S(2)}, u32[]{:S(2)}) collective-permute-start(f32[256,513]{0,1:T(8,128)} %get-tuple-element.2179), channel_id=1, source_target_pairs={{1,0},{2,1},{3,2},{4,3},{5,4},{6,5},{7,6},{8,7},{9,8},{10,9},{11,1... | collective-permute-start | bytes 1575944 | tf_op jit(solution)/shard_map/ppermute | solution.py:18
  211.3 23.8 %collective-permute-start.3 = (f32[256,513]{0,1:T(8,128)}, f32[256,513]{0,1:T(8,128)S(1)}, u32[]{:S(2)}, u32[]{:S(2)}) collective-permute-start(f32[256,513]{0,1:T(8,128)} %get-tuple-element.2180), channel_id=1, source_target_pairs={{0,2},{1,3},{2,4},{3,5},{4,6},{5,7},{6,8},{7,9},{8,10},{9,11},{10,... | collective-permute-start | bytes 1575944 | tf_op jit(solution)/shard_map/ppermute | solution.py:18
  217.0 19.6 %collective-permute-start.4 = (f32[256,513]{0,1:T(8,128)}, f32[256,513]{0,1:T(8,128)}, u32[]{:S(2)}, u32[]{:S(2)}) collective-permute-start(f32[256,513]{0,1:T(8,128)} %get-tuple-element.2180), channel_id=1, source_target_pairs={{2,0},{3,1},{4,2},{5,3},{6,4},{7,5},{8,6},{9,7},{10,8},{11,9},{12,... | collective-permute-start | bytes 1575944 | tf_op jit(solution)/shard_map/ppermute | solution.py:18
  260.5 23.4 %collective-permute-start.5 = (f32[256,513]{0,1:T(8,128)}, f32[256,513]{0,1:T(8,128)S(1)}, u32[]{:S(2)}, u32[]{:S(2)}) collective-permute-start(f32[256,513]{0,1:T(8,128)} %get-tuple-element.2181), channel_id=1, source_target_pairs={{0,4},{1,5},{2,6},{3,7},{4,8},{5,9},{6,10},{7,11},{8,12},{9,13},{1... | collective-permute-start | bytes 1575944 | tf_op jit(solution)/shard_map/ppermute | solution.py:18
  263.9 21.2 %collective-permute-start.6 = (f32[256,513]{0,1:T(8,128)}, f32[256,513]{0,1:T(8,128)}, u32[]{:S(2)}, u32[]{:S(2)}) collective-permute-start(f32[256,513]{0,1:T(8,128)} %get-tuple-element.2181), channel_id=1, source_target_pairs={{4,0},{5,1},{6,2},{7,3},{8,4},{9,5},{10,6},{11,7},{12,8},{13,9},{1... | collective-permute-start | bytes 1575944 | tf_op jit(solution)/shard_map/ppermute | solution.py:18
  316.8 22.3 %collective-permute-start.7 = (f32[256,513]{0,1:T(8,128)}, f32[256,513]{0,1:T(8,128)S(1)}, u32[]{:S(2)}, u32[]{:S(2)}) collective-permute-start(f32[256,513]{0,1:T(8,128)} %get-tuple-element.2182), channel_id=1, source_target_pairs={{0,8},{1,9},{2,10},{3,11},{4,12},{5,13},{6,14},{7,15},{8,16},{9,17... | collective-permute-start | bytes 1575944 | tf_op jit(solution)/shard_map/ppermute | solution.py:18
  318.2 22.1 %collective-permute-start.8 = (f32[256,513]{0,1:T(8,128)}, f32[256,513]{0,1:T(8,128)}, u32[]{:S(2)}, u32[]{:S(2)}) collective-permute-start(f32[256,513]{0,1:T(8,128)} %get-tuple-element.2182), channel_id=1, source_target_pairs={{8,0},{9,1},{10,2},{11,3},{12,4},{13,5},{14,6},{15,7},{16,8},{17,9... | collective-permute-start | bytes 1575944 | tf_op jit(solution)/shard_map/ppermute | solution.py:18
  374.9 20.7 %collective-permute-start.9 = (f32[256,513]{0,1:T(8,128)}, f32[256,513]{0,1:T(8,128)S(1)}, u32[]{:S(2)}, u32[]{:S(2)}) collective-permute-start(f32[256,513]{0,1:T(8,128)} %get-tuple-element.2183), channel_id=1, source_target_pairs={{0,16},{1,17},{2,18},{3,19},{4,20},{5,21},{6,22},{7,23},{8,24},{9,... | collective-permute-start | bytes 1575944 | tf_op jit(solution)/shard_map/ppermute | solution.py:18
  379.1 22.8 %collective-permute-start.10 = (f32[256,513]{0,1:T(8,128)}, f32[256,513]{0,1:T(8,128)}, u32[]{:S(2)}, u32[]{:S(2)}) collective-permute-start(f32[256,513]{0,1:T(8,128)} %get-tuple-element.2183), channel_id=1, source_target_pairs={{16,0},{17,1},{18,2},{19,3},{20,4},{21,5},{22,6},{23,7},{24,8},{25... | collective-permute-start | bytes 1575944 | tf_op jit(solution)/shard_map/ppermute | solution.py:18
  436.6 27.7 %collective-permute-start.11 = (f32[256,513]{0,1:T(8,128)}, f32[256,513]{0,1:T(8,128)S(1)}, u32[]{:S(2)}, u32[]{:S(2)}) collective-permute-start(f32[256,513]{0,1:T(8,128)} %get-tuple-element.2184), channel_id=1, source_target_pairs={{0,32},{1,33},{2,34},{3,35},{4,36},{5,37},{6,38},{7,39},{8,40},{9,... | collective-permute-start | bytes 1575944 | tf_op jit(solution)/shard_map/ppermute | solution.py:18
  462.5 11.6 %collective-permute-start.12 = (f32[256,513]{0,1:T(8,128)}, f32[256,513]{0,1:T(8,128)}, u32[]{:S(2)}, u32[]{:S(2)}) collective-permute-start(f32[256,513]{0,1:T(8,128)} %get-tuple-element.2184), channel_id=1, source_target_pairs={{32,0},{33,1},{34,2},{35,3},{36,4},{37,5},{38,6},{39,7},{40,8},{41... | collective-permute-start | bytes 1575944 | tf_op jit(solution)/shard_map/ppermute | solution.py:18
  508.7 17.0 %collective-permute-start.13 = (f32[256,513]{0,1:T(8,128)}, f32[256,513]{0,1:T(8,128)S(1)}, u32[]{:S(2)}, u32[]{:S(2)}) collective-permute-start(f32[256,513]{0,1:T(8,128)} %get-tuple-element.2185), channel_id=1, source_target_pairs={{0,64},{1,65},{2,66},{3,67},{4,68},{5,69},{6,70},{7,71},{8,72},{9,... | collective-permute-start | bytes 1575944 | tf_op jit(solution)/shard_map/ppermute | solution.py:18
  514.9 16.8 %collective-permute-start.14 = (f32[256,513]{0,1:T(8,128)}, f32[256,513]{0,1:T(8,128)}, u32[]{:S(2)}, u32[]{:S(2)}) collective-permute-start(f32[256,513]{0,1:T(8,128)} %get-tuple-element.2185), channel_id=1, source_target_pairs={{64,0},{65,1},{66,2},{67,3},{68,4},{69,5},{70,6},{71,7},{72,8},{73... | collective-permute-start | bytes 1575944 | tf_op jit(solution)/shard_map/ppermute | solution.py:18
  564.8 14.2 %collective-permute-start.15 = (f32[256,513]{0,1:T(8,128)S(1)}, f32[256,513]{0,1:T(8,128)S(1)}, u32[]{:S(2)}, u32[]{:S(2)}) collective-permute-start(f32[256,513]{0,1:T(8,128)S(1)} %get-tuple-element.2186), channel_id=1, source_target_pairs={{0,128},{1,129},{2,130},{3,131},{4,132},{5,133},{6,134},{7,135},{8... | collective-permute-start | bytes 1575944 | tf_op jit(solution)/shard_map/ppermute | solution.py:18
  568.1 16.7 %collective-permute-start.16 = (f32[256,513]{0,1:T(8,128)S(1)}, f32[256,513]{0,1:T(8,128)}, u32[]{:S(2)}, u32[]{:S(2)}) collective-permute-start(f32[256,513]{0,1:T(8,128)S(1)} %get-tuple-element.2186), channel_id=1, source_target_pairs={{128,0},{129,1},{130,2},{131,3},{132,4},{133,5},{134,6},{135,7},{1... | collective-permute-start | bytes 1575944 | tf_op jit(solution)/shard_map/ppermute | solution.py:18
  611.4 7.6 %collective-permute-start.17 = (f32[256]{0:T(256)S(1)}, f32[256]{0:T(256)S(1)}, u32[]{:S(2)}, u32[]{:S(2)}) collective-permute-start(f32[256]{0:T(256)S(1)} %get-tuple-element.521), channel_id=1, source_target_pairs={{0,1},{1,2},{2,3},{3,4},{4,5},{5,6},{6,7},{7,8},{8,9},{9,10},{10,1... | collective-permute-start | bytes 3080 | tf_op jit(solution)/shard_map/ppermute | solution.py:18
Sparse Core Ops, SparseCore 0:
  76.1 43.4 reduce-scatter.1

commit v2 on v1

--- a/solution.py
+++ b/solution.py
@@ -19,18 +19,21 @@
 
 
 def regressors(frames_flat, link_rows, lag_steps, topology):
-    samples = frames_flat.shape[0]
-    frames = frames_flat.reshape(samples, WIN, GROUPS)
-    picker = (
-        lax.broadcasted_iota(jnp.int32, (NLAG, WIN), 1) == (WIN - 1 - lag_steps)[:, None]
-    ).astype(jnp.bfloat16)
-    lagged = jnp.einsum("lw,swg->slg", picker, frames, preferred_element_type=jnp.float32)
+    samples, feats = frames_flat.shape
+    columns = NLAG * GROUPS
+    source = lax.broadcasted_iota(jnp.int32, (feats, columns), 0)
+    target_col = lax.broadcasted_iota(jnp.int32, (feats, columns), 1)
+    lag_of_col = jnp.repeat(lag_steps, GROUPS, total_repeat_length=columns)
+    wanted = (WIN - 1 - lag_of_col)[None, :] * GROUPS + target_col % GROUPS
+    picker = (source == wanted).astype(jnp.bfloat16)
+    lagged = jnp.dot(frames_flat, picker, preferred_element_type=jnp.float32)
     chosen = (link_rows[:, None] == lax.broadcasted_iota(jnp.int32, (samples, GROUPS), 1)).astype(
         jnp.bfloat16
     )
     neighbour = jnp.dot(chosen, topology.astype(jnp.bfloat16), preferred_element_type=jnp.float32)
-    design = (lagged * neighbour[:, None, :]).reshape(samples, NLAG * GROUPS).astype(jnp.bfloat16)
-    target = jnp.sum(frames[:, WIN - 1, :].astype(jnp.float32) * chosen.astype(jnp.float32), axis=1)
+    design = (lagged * jnp.tile(neighbour, (1, NLAG))).astype(jnp.bfloat16)
+    latest = frames_flat[:, (WIN - 1) * GROUPS :].astype(jnp.float32)
+    target = jnp.sum(latest * chosen.astype(jnp.float32), axis=1)
     return (design, target)
 
 
@@ -106,17 +109,28 @@
     design, target = regressors(
         window.reshape(samples, feats), link_ids.reshape(samples), lag_steps, topology
     )
-    knot_flat = knot_ids.reshape(samples)
-    group_span = KPD * n_tm
-    knot_slot = knot_flat // group_span * KPD + knot_flat % KPD
-    packed = lax.psum_scatter(
-        slot_terms(design, target, knot_slot, KPD * lax.axis_size("dp")),
-        "dp",
-        scatter_dimension=0,
-        tiled=True,
+    dest = dp_rows // n_dp
+    by_owner = design.reshape(tm_rows, n_dp, dest, columns).transpose(1, 0, 2, 3)
+    parity = (knot_ids.reshape(samples) % KPD).astype(jnp.float32)
+    side = jnp.stack([target, parity], 0).reshape(2, tm_rows, n_dp, dest).transpose(2, 0, 1, 3)
+    got = lax.all_to_all(
+        by_owner.reshape(n_dp, tm_rows * dest, columns), "dp", 0, 0, tiled=True
+    ).reshape(samples, columns)
+    got_side = lax.all_to_all(
+        side.reshape(n_dp, 2, tm_rows * dest), "dp", 0, 0, tiled=True
     )
-    grams = packed[:, :columns, :] / per_knot
-    moments = packed[:, columns, :] / per_knot
+    got_target = got_side[:, 0, :].reshape(samples)
+    got_parity = got_side[:, 1, :].reshape(samples)
+    grams = []
+    moments = []
+    for which in range(KPD):
+        weight = (got_parity == which).astype(jnp.bfloat16)
+        weighted = got * weight[:, None]
+        grams.append(
+            jnp.einsum("sa,sb->ab", weighted, got, preferred_element_type=jnp.float32) / per_knot
+        )
+        scaled_target = (got_target * weight.astype(jnp.float32)).astype(jnp.bfloat16)
+        moments.append(jnp.dot(scaled_target, got, preferred_element_type=jnp.float32) / per_knot)
     identity = jnp.eye(columns, dtype=jnp.float32)
     penalty_diag = jnp.diag(smooth)
     has_left = (device > 0).astype(jnp.float32)

time: 637 us -> 532 us (0.84)
  the two profiles are of different devices: /device:TPU:32 before, /device:TPU:24 now
where the time goes in v2:
time: 532 us; the launch traced here: 522 us
  waiting for transfers between devices  174 us (33%)
  loops' own time  96.5 us (18%)
  matrix products  95.9 us (18%)
  starting transfers between devices  75.2 us (14%)
  local copies, waits for them, and re-layouts  42.9 us (8%)
  between operations  21.7 us (4%)
  other arithmetic  15.9 us (3%)
    ppermute x18, waiting for transfers between devices, from_behind(): return lax.ppermute(block, axis, route)  160 us
    dot_general x118, matrix products, dense_dot(): return jnp.dot(left_mat, right_mat, precision=lax.Precision.HIGHEST)  90.8 us
    ppermute x18, starting transfers between devices, from_behind(): return lax.ppermute(block, axis, route)  65.2 us
    another operation x10, loops' own time, solve_spd(): lax.while_loop(going, refine, (start, gap0, norm0, 0))  58.1 us
    another operation x10, loops' own time, solve_spd(): lax.cond(norm2 <= NS_TOL2, lambda: quick, lambda: cholesky_solve(matrix,...  38.4 us
    gather x10, local copies, waits for them, and re-layouts, solve_spd(): inv_diag = 1.0 / jnp.diagonal(matrix)  23.7 us
    all_to_all x1, waiting for transfers between devices, body(): lax.all_to_all(by_owner.reshape(n_dp, tm_rows * dest, columns), 'dp', 0,...  13.7 us
  transfers between devices with their start and end apart: 20, of which 19 were waited for; matrix products, arithmetic and copies ran while one was open for 4% of the time, Pallas kernels for 0%

profile of v2, /device:TPU:24, one launch (start us, length us, event | category | flops | bytes accessed | tf_op | source)
XLA Modules:
  0.0 522.2 jit_solution(14966585099160669156)
XLA Ops:
  4.6 5.2 all-to-all-start.1
  26.1 13.7 %all-to-all-done = bf16[8,256,256]{1,2,0:T(8,128)(2,1)S(1)} async-done(((bf16[8,256,256]{1,2,0:T(8,128)(2,1)}), bf16[8,256,256]{1,2,0:T(8,128)(2,1)S(1)}, u32[]{:S(2)}, u32[]{:S(2)}) %all-to-all-start) | async-done | bytes 1048608 | tf_op jit(solution)/shard_map/all_to_all | solution.py:116
  54.1 5.3 %conditional.10 = (f32[256,513]{0,1:T(8,128)S(1)}) conditional(s32[]{:T(128)} %convert_element_type.170, (f32[256,256]{0,1:T(8,128)S(1)}, f32[256,513]{0,1:T(8,128)}) %tuple.120, f32[256,513]{0,1:T(8,128)} %fusion.258), branch_computations={%region_8.15_spmd, %region_13.16_spmd} | conditional | flops 656294656 | bytes 10465515 | solution.py:89
  59.4 8.2 %collective-permute-start = (f32[256,513]{0,1:T(8,128)S(1)}, f32[256,513]{0,1:T(8,128)S(1)}, u32[]{:S(2)}, u32[]{:S(2)}) collective-permute-start(f32[256,513]{0,1:T(8,128)S(1)} %get-tuple-element.2275), channel_id=1, source_target_pairs={{1,0},{2,1},{3,2},{4,3},{5,4},{6,5},{7,6},{8,7},{9,8},{10,9},{11,1... | collective-permute-start | bytes 1575944 | tf_op jit(solution)/shard_map/ppermute | solution.py:18
  68.5 10.9 %collective-permute-done = f32[256,513]{0,1:T(8,128)S(1)} collective-permute-done((f32[256,513]{0,1:T(8,128)S(1)}, f32[256,513]{0,1:T(8,128)S(1)}, u32[]{:S(2)}, u32[]{:S(2)}) %collective-permute-start) | collective-permute-done | bytes 525344 | tf_op jit(solution)/shard_map/ppermute | solution.py:18
  97.4 8.0 %collective-permute-start.2 = (f32[256,513]{0,1:T(8,128)S(1)}, f32[256,513]{0,1:T(8,128)S(1)}, u32[]{:S(2)}, u32[]{:S(2)}) collective-permute-start(f32[256,513]{0,1:T(8,128)S(1)} %get-tuple-element.2276), channel_id=1, source_target_pairs={{1,0},{2,1},{3,2},{4,3},{5,4},{6,5},{7,6},{8,7},{9,8},{10,9},{11,1... | collective-permute-start | bytes 1575944 | tf_op jit(solution)/shard_map/ppermute | solution.py:18
  107.3 10.3 %collective-permute-done.2 = f32[256,513]{0,1:T(8,128)S(1)} collective-permute-done((f32[256,513]{0,1:T(8,128)S(1)}, f32[256,513]{0,1:T(8,128)S(1)}, u32[]{:S(2)}, u32[]{:S(2)}) %collective-permute-start.2) | collective-permute-done | bytes 525344 | tf_op jit(solution)/shard_map/ppermute | solution.py:18
  138.4 5.0 conditional.12
  145.3 5.4 %collective-permute-start.3 = (f32[256,513]{0,1:T(8,128)S(1)}, f32[256,513]{0,1:T(8,128)S(1)}, u32[]{:S(2)}, u32[]{:S(2)}) collective-permute-start(f32[256,513]{0,1:T(8,128)S(1)} %get-tuple-element.2277), channel_id=1, source_target_pairs={{0,2},{1,3},{2,4},{3,5},{4,6},{5,7},{6,8},{7,9},{8,10},{9,11},{10,... | collective-permute-start | bytes 1575944 | tf_op jit(solution)/shard_map/ppermute | solution.py:18
  150.8 11.8 %collective-permute-done.4 = f32[256,513]{0,1:T(8,128)} collective-permute-done((f32[256,513]{0,1:T(8,128)S(1)}, f32[256,513]{0,1:T(8,128)}, u32[]{:S(2)}, u32[]{:S(2)}) %collective-permute-start.4) | collective-permute-done | bytes 525344 | tf_op jit(solution)/shard_map/ppermute | solution.py:18
  172.1 6.7 %while.183 = (f32[256,256]{1,0:T(8,128)S(1)}, f32[256,256]{1,0:T(8,128)S(1)}, f32[]{:T(128)}, s32[]{:T(128)}, f32[256,256]{1,0:T(8,128)S(1)}, /*index=5*/s32[]{:T(128)}) while((f32[256,256]{1,0:T(8,128)S(1)}, f32[256,256]{1,0:T(8,128)S(1)}, f32[]{:T(128)}, s32[]{:T(128)}, f32[256,256]{1,0:T(8,128)S(1)}, ...), condition=%wide.region_38.41_spmd.clone, body=%wide.region_36.40_spmd.clone.sunk | while | flops 403046400 | bytes 2097245 | solution.py:86
  181.4 5.3 %conditional.13 = (f32[256,513]{0,1:T(8,128)S(1)}) conditional(s32[]{:T(128)} %convert_element_type.184, (f32[256,256]{0,1:T(8,128)S(1)}, f32[256,513]{0,1:T(8,128)S(1)}) %tuple.126, f32[256,513]{0,1:T(8,128)} %fusion.255), branch_computations={%region_39.42_spmd, %region_40.43_spmd} | conditional | flops 656294656 | bytes 8363223 | solution.py:89
  192.8 9.9 %collective-permute-done.6 = f32[256,513]{0,1:T(8,128)} collective-permute-done((f32[256,513]{0,1:T(8,128)S(1)}, f32[256,513]{0,1:T(8,128)}, u32[]{:S(2)}, u32[]{:S(2)}) %collective-permute-start.6) | collective-permute-done | bytes 525344 | tf_op jit(solution)/shard_map/ppermute | solution.py:18
  215.3 12.1 %while.184 = (f32[256,256]{1,0:T(8,128)S(1)}, f32[256,256]{1,0:T(8,128)S(1)}, f32[]{:T(128)}, s32[]{:T(128)}, f32[256,256]{1,0:T(8,128)S(1)}, /*index=5*/s32[]{:T(128)}) while((f32[256,256]{1,0:T(8,128)S(1)}, f32[256,256]{1,0:T(8,128)S(1)}, f32[]{:T(128)}, s32[]{:T(128)}, f32[256,256]{1,0:T(8,128)S(1)}, ...), condition=%wide.region_47.50_spmd.clone, body=%wide.region_45.49_spmd.clone.sunk | while | flops 403046400 | bytes 2097245 | solution.py:86
  240.8 16.1 %collective-permute-done.8 = f32[256,513]{0,1:T(8,128)S(1)} collective-permute-done((f32[256,513]{0,1:T(8,128)}, f32[256,513]{0,1:T(8,128)S(1)}, u32[]{:S(2)}, u32[]{:S(2)}) %collective-permute-start.8) | collective-permute-done | bytes 525344 | tf_op jit(solution)/shard_map/ppermute | solution.py:18
  257.6 7.8 %collective-permute-done.7 = f32[256,513]{0,1:T(8,128)S(1)} collective-permute-done((f32[256,513]{0,1:T(8,128)}, f32[256,513]{0,1:T(8,128)S(1)}, u32[]{:S(2)}, u32[]{:S(2)}) %collective-permute-start.7) | collective-permute-done | bytes 525344 | tf_op jit(solution)/shard_map/ppermute | solution.py:18
  271.9 14.9 %while.185 = (f32[256,256]{1,0:T(8,128)S(1)}, f32[256,256]{1,0:T(8,128)S(1)}, f32[]{:T(128)}, s32[]{:T(128)}, f32[256,256]{1,0:T(8,128)S(1)}, /*index=5*/s32[]{:T(128)}) while((f32[256,256]{1,0:T(8,128)S(1)}, f32[256,256]{1,0:T(8,128)S(1)}, f32[]{:T(128)}, s32[]{:T(128)}, f32[256,256]{1,0:T(8,128)S(1)}, ...), condition=%wide.region_56.59_spmd.clone, body=%wide.region_54.58_spmd.clone.sunk | while | flops 403046400 | bytes 2097245 | solution.py:86
  289.3 5.3 %conditional.15 = (f32[256,513]{0,1:T(8,128)S(1)}) conditional(s32[]{:T(128)} %convert_element_type.186, (f32[256,256]{0,1:T(8,128)S(1)}, f32[256,513]{0,1:T(8,128)S(1)}) %tuple.130, f32[256,513]{0,1:T(8,128)} %fusion.253), branch_computations={%region_57.60_spmd, %region_58.61_spmd} | conditional | flops 656294656 | bytes 8363223 | solution.py:89
  297.0 7.3 %collective-permute-start.9 = (f32[256,513]{0,1:T(8,128)S(1)}, f32[256,513]{0,1:T(8,128)}, u32[]{:S(2)}, u32[]{:S(2)}) collective-permute-start(f32[256,513]{0,1:T(8,128)S(1)} %get-tuple-element.2280), channel_id=1, source_target_pairs={{0,16},{1,17},{2,18},{3,19},{4,20},{5,21},{6,22},{7,23},{8,24},{9,... | collective-permute-start | bytes 1575944 | tf_op jit(solution)/shard_map/ppermute | solution.py:18
  304.3 11.0 %collective-permute-done.10 = f32[256,513]{0,1:T(8,128)} collective-permute-done((f32[256,513]{0,1:T(8,128)S(1)}, f32[256,513]{0,1:T(8,128)}, u32[]{:S(2)}, u32[]{:S(2)}) %collective-permute-start.10) | collective-permute-done | bytes 525344 | tf_op jit(solution)/shard_map/ppermute | solution.py:18
  317.0 31.4 %collective-permute-done.9 = f32[256,513]{0,1:T(8,128)} collective-permute-done((f32[256,513]{0,1:T(8,128)S(1)}, f32[256,513]{0,1:T(8,128)}, u32[]{:S(2)}, u32[]{:S(2)}) %collective-permute-start.9) | collective-permute-done | bytes 525344 | tf_op jit(solution)/shard_map/ppermute | solution.py:18
  356.1 14.9 %while.186 = (f32[256,256]{1,0:T(8,128)S(1)}, f32[256,256]{1,0:T(8,128)S(1)}, f32[]{:T(128)}, s32[]{:T(128)}, f32[256,256]{1,0:T(8,128)S(1)}, /*index=5*/s32[]{:T(128)}) while((f32[256,256]{1,0:T(8,128)S(1)}, f32[256,256]{1,0:T(8,128)S(1)}, f32[]{:T(128)}, s32[]{:T(128)}, f32[256,256]{1,0:T(8,128)S(1)}, ...), condition=%wide.region_65.68_spmd.clone, body=%wide.region_63.67_spmd.clone.sunk | while | flops 403046400 | bytes 2097245 | solution.py:86
  381.9 5.0 collective-permute-done.12
  387.6 5.5 %collective-permute-done.11 = f32[256,513]{0,1:T(8,128)S(1)} collective-permute-done((f32[256,513]{0,1:T(8,128)}, f32[256,513]{0,1:T(8,128)S(1)}, u32[]{:S(2)}, u32[]{:S(2)}) %collective-permute-start.11) | collective-permute-done | bytes 525344 | tf_op jit(solution)/shard_map/ppermute | solution.py:18
  399.7 14.9 %while.187 = (f32[256,256]{1,0:T(8,128)S(1)}, f32[256,256]{1,0:T(8,128)S(1)}, f32[]{:T(128)}, s32[]{:T(128)}, f32[256,256]{1,0:T(8,128)S(1)}, /*index=5*/s32[]{:T(128)}) while((f32[256,256]{1,0:T(8,128)S(1)}, f32[256,256]{1,0:T(8,128)S(1)}, f32[]{:T(128)}, s32[]{:T(128)}, f32[256,256]{1,0:T(8,128)S(1)}, ...), condition=%wide.region_74.77_spmd.clone, body=%wide.region_72.76_spmd.clone.sunk | while | flops 403046400 | bytes 2097245 | solution.py:86
  417.1 5.3 %conditional.17 = (f32[256,513]{0,1:T(8,128)S(1)}) conditional(s32[]{:T(128)} %convert_element_type.188, (f32[256,256]{0,1:T(8,128)S(1)}, f32[256,513]{0,1:T(8,128)S(1)}) %tuple.134, f32[256,513]{0,1:T(8,128)} %fusion.251), branch_computations={%region_75.78_spmd, %region_76.79_spmd} | conditional | flops 656294656 | bytes 8363223 | solution.py:89
  428.0 7.6 %collective-permute-done.14 = f32[256,513]{0,1:T(8,128)} collective-permute-done((f32[256,513]{0,1:T(8,128)S(1)}, f32[256,513]{0,1:T(8,128)}, u32[]{:S(2)}, u32[]{:S(2)}) %collective-permute-start.14) | collective-permute-done | bytes 525344 | tf_op jit(solution)/shard_map/ppermute | solution.py:18
  448.2 14.9 %while.188 = (f32[256,256]{1,0:T(8,128)S(1)}, f32[256,256]{1,0:T(8,128)S(1)}, f32[]{:T(128)}, s32[]{:T(128)}, f32[256,256]{1,0:T(8,128)S(1)}, /*index=5*/s32[]{:T(128)}) while((f32[256,256]{1,0:T(8,128)S(1)}, f32[256,256]{1,0:T(8,128)S(1)}, f32[]{:T(128)}, s32[]{:T(128)}, f32[256,256]{1,0:T(8,128)S(1)}, ...), condition=%wide.region_83.86_spmd.clone, body=%wide.region_81.85_spmd.clone.sunk | while | flops 403046400 | bytes 2097245 | solution.py:86
  473.0 9.1 %collective-permute-done.16 = f32[256,513]{0,1:T(8,128)S(1)} collective-permute-done((f32[256,513]{0,1:T(8,128)S(1)}, f32[256,513]{0,1:T(8,128)S(1)}, u32[]{:S(2)}, u32[]{:S(2)}) %collective-permute-start.16) | collective-permute-done | bytes 525344 | tf_op jit(solution)/shard_map/ppermute | solution.py:18
  482.7 5.0 collective-permute-done.15
  494.4 14.9 %while.189 = (f32[256,256]{1,0:T(8,128)S(1)}, f32[256,256]{1,0:T(8,128)S(1)}, f32[]{:T(128)}, s32[]{:T(128)}, f32[256,256]{1,0:T(8,128)S(1)}, /*index=5*/s32[]{:T(128)}) while((f32[256,256]{1,0:T(8,128)S(1)}, f32[256,256]{1,0:T(8,128)S(1)}, f32[]{:T(128)}, s32[]{:T(128)}, f32[256,256]{1,0:T(8,128)S(1)}, ...), condition=%wide.region_92.95_spmd.clone, body=%wide.region_90.94_spmd.clone.sunk | while | flops 403046400 | bytes 2097245 | solution.py:86
  514.9 6.1 %collective-permute-done.17 = f32[256]{0:T(256)S(1)} collective-permute-done((f32[256]{0:T(256)S(1)}, f32[256]{0:T(256)S(1)}, u32[]{:S(2)}, u32[]{:S(2)}) %collective-permute-start.17) | collective-permute-done | bytes 1056 | tf_op jit(solution)/shard_map/ppermute | solution.py:18
  (442 shorter events, 239.8 us)
Async XLA Ops:
  4.6 16.6 %all-to-all-start.1 = ((f32[8,2,256]{2,1,0:T(2,128)}), f32[8,2,256]{2,1,0:T(2,128)S(1)}, u32[]{:S(2)}, u32[]{:S(2)}) async-start(f32[8,2,256]{2,1,0:T(2,128)} %reshape.531), calls=%async_computation.1 | async-start | bytes 32768 | tf_op jit(solution)/shard_map/all_to_all | solution.py:119
  21.2 18.7 %all-to-all-start = ((bf16[8,256,256]{1,2,0:T(8,128)(2,1)}), bf16[8,256,256]{1,2,0:T(8,128)(2,1)S(1)}, u32[]{:S(2)}, u32[]{:S(2)}) async-start(bf16[8,256,256]{1,2,0:T(8,128)(2,1)} %copy.212), calls=%async_computation | async-start | bytes 2097152 | tf_op jit(solution)/shard_map/all_to_all | solution.py:116
  59.4 20.0 %collective-permute-start = (f32[256,513]{0,1:T(8,128)S(1)}, f32[256,513]{0,1:T(8,128)S(1)}, u32[]{:S(2)}, u32[]{:S(2)}) collective-permute-start(f32[256,513]{0,1:T(8,128)S(1)} %get-tuple-element.2275), channel_id=1, source_target_pairs={{1,0},{2,1},{3,2},{4,3},{5,4},{6,5},{7,6},{8,7},{9,8},{10,9},{11,1... | collective-permute-start | bytes 1575944 | tf_op jit(solution)/shard_map/ppermute | solution.py:18
  97.4 20.3 %collective-permute-start.2 = (f32[256,513]{0,1:T(8,128)S(1)}, f32[256,513]{0,1:T(8,128)S(1)}, u32[]{:S(2)}, u32[]{:S(2)}) collective-permute-start(f32[256,513]{0,1:T(8,128)S(1)} %get-tuple-element.2276), channel_id=1, source_target_pairs={{1,0},{2,1},{3,2},{4,3},{5,4},{6,5},{7,6},{8,7},{9,8},{10,9},{11,1... | collective-permute-start | bytes 1575944 | tf_op jit(solution)/shard_map/ppermute | solution.py:18
  105.4 18.8 %collective-permute-start.1 = (f32[256,513]{0,1:T(8,128)S(1)}, f32[256,513]{0,1:T(8,128)S(1)}, u32[]{:S(2)}, u32[]{:S(2)}) collective-permute-start(f32[256,513]{0,1:T(8,128)S(1)} %get-tuple-element.2276), channel_id=1, source_target_pairs={{0,1},{1,2},{2,3},{3,4},{4,5},{5,6},{6,7},{7,8},{8,9},{9,10},{10,1... | collective-permute-start | bytes 1575944 | tf_op jit(solution)/shard_map/ppermute | solution.py:18
  138.4 24.2 %copy-start.1 = (f32[256,513]{0,1:T(8,128)S(1)}, f32[256,513]{0,1:T(8,128)}, u32[]{:S(2)}) copy-start(f32[256,513]{0,1:T(8,128)} %copy-done) | copy-start | bytes 1575940
  138.4 27.3 %copy-start.3 = (f32[256,513]{0,1:T(8,128)S(1)}, f32[256,513]{0,1:T(8,128)}, u32[]{:S(2)}) copy-start(f32[256,513]{0,1:T(8,128)} %copy-done.2) | copy-start | bytes 1575940
  143.4 19.1 %collective-permute-start.4 = (f32[256,513]{0,1:T(8,128)S(1)}, f32[256,513]{0,1:T(8,128)}, u32[]{:S(2)}, u32[]{:S(2)}) collective-permute-start(f32[256,513]{0,1:T(8,128)S(1)} %get-tuple-element.2277), channel_id=1, source_target_pairs={{2,0},{3,1},{4,2},{5,3},{6,4},{7,5},{8,6},{9,7},{10,8},{11,9},{12,... | collective-permute-start | bytes 1575944 | tf_op jit(solution)/shard_map/ppermute | solution.py:18
  145.3 20.3 %collective-permute-start.3 = (f32[256,513]{0,1:T(8,128)S(1)}, f32[256,513]{0,1:T(8,128)S(1)}, u32[]{:S(2)}, u32[]{:S(2)}) collective-permute-start(f32[256,513]{0,1:T(8,128)S(1)} %get-tuple-element.2277), channel_id=1, source_target_pairs={{0,2},{1,3},{2,4},{3,5},{4,6},{5,7},{6,8},{7,9},{8,10},{9,11},{10,... | collective-permute-start | bytes 1575944 | tf_op jit(solution)/shard_map/ppermute | solution.py:18
  181.4 21.3 %copy-start.5 = (f32[256,513]{0,1:T(8,128)S(1)}, f32[256,513]{0,1:T(8,128)}, u32[]{:S(2)}) copy-start(f32[256,513]{0,1:T(8,128)} %copy-done.4) | copy-start | bytes 1575940
  181.4 26.2 %copy-start.7 = (f32[256,513]{0,1:T(8,128)S(1)}, f32[256,513]{0,1:T(8,128)}, u32[]{:S(2)}) copy-start(f32[256,513]{0,1:T(8,128)} %copy-done.6) | copy-start | bytes 1575940
  186.7 16.0 %collective-permute-start.6 = (f32[256,513]{0,1:T(8,128)S(1)}, f32[256,513]{0,1:T(8,128)}, u32[]{:S(2)}, u32[]{:S(2)}) collective-permute-start(f32[256,513]{0,1:T(8,128)S(1)} %get-tuple-element.2278), channel_id=1, source_target_pairs={{4,0},{5,1},{6,2},{7,3},{8,4},{9,5},{10,6},{11,7},{12,8},{13,9},{1... | collective-permute-start | bytes 1575944 | tf_op jit(solution)/shard_map/ppermute | solution.py:18
  190.9 16.8 %collective-permute-start.5 = (f32[256,513]{0,1:T(8,128)S(1)}, f32[256,513]{0,1:T(8,128)}, u32[]{:S(2)}, u32[]{:S(2)}) collective-permute-start(f32[256,513]{0,1:T(8,128)S(1)} %get-tuple-element.2278), channel_id=1, source_target_pairs={{0,4},{1,5},{2,6},{3,7},{4,8},{5,9},{6,10},{7,11},{8,12},{9,13},{1... | collective-permute-start | bytes 1575944 | tf_op jit(solution)/shard_map/ppermute | solution.py:18
  229.2 27.7 %copy-start.9 = (f32[256,513]{0,1:T(8,128)S(1)}, f32[256,513]{0,1:T(8,128)}, u32[]{:S(2)}) copy-start(f32[256,513]{0,1:T(8,128)} %copy-done.8) | copy-start | bytes 1575940
  229.3 36.1 %copy-start.11 = (f32[256,513]{0,1:T(8,128)S(1)}, f32[256,513]{0,1:T(8,128)}, u32[]{:S(2)}) copy-start(f32[256,513]{0,1:T(8,128)} %copy-done.10) | copy-start | bytes 1575940
  234.1 22.9 %collective-permute-start.8 = (f32[256,513]{0,1:T(8,128)}, f32[256,513]{0,1:T(8,128)S(1)}, u32[]{:S(2)}, u32[]{:S(2)}) collective-permute-start(f32[256,513]{0,1:T(8,128)} %get-tuple-element.2279), channel_id=1, source_target_pairs={{8,0},{9,1},{10,2},{11,3},{12,4},{13,5},{14,6},{15,7},{16,8},{17,9... | collective-permute-start | bytes 1575944 | tf_op jit(solution)/shard_map/ppermute | solution.py:18
  236.0 29.4 %collective-permute-start.7 = (f32[256,513]{0,1:T(8,128)}, f32[256,513]{0,1:T(8,128)S(1)}, u32[]{:S(2)}, u32[]{:S(2)}) collective-permute-start(f32[256,513]{0,1:T(8,128)} %get-tuple-element.2279), channel_id=1, source_target_pairs={{0,8},{1,9},{2,10},{3,11},{4,12},{5,13},{6,14},{7,15},{8,16},{9,17... | collective-permute-start | bytes 1575944 | tf_op jit(solution)/shard_map/ppermute | solution.py:18
  289.3 26.1 %copy-start.13 = (f32[256,513]{0,1:T(8,128)S(1)}, f32[256,513]{0,1:T(8,128)}, u32[]{:S(2)}) copy-start(f32[256,513]{0,1:T(8,128)} %copy-done.12) | copy-start | bytes 1575940
  289.3 59.1 %copy-start.15 = (f32[256,513]{0,1:T(8,128)S(1)}, f32[256,513]{0,1:T(8,128)}, u32[]{:S(2)}) copy-start(f32[256,513]{0,1:T(8,128)} %copy-done.14) | copy-start | bytes 1575940
  294.6 20.8 %collective-permute-start.10 = (f32[256,513]{0,1:T(8,128)S(1)}, f32[256,513]{0,1:T(8,128)}, u32[]{:S(2)}, u32[]{:S(2)}) collective-permute-start(f32[256,513]{0,1:T(8,128)S(1)} %get-tuple-element.2280), channel_id=1, source_target_pairs={{16,0},{17,1},{18,2},{19,3},{20,4},{21,5},{22,6},{23,7},{24,8},{25... | collective-permute-start | bytes 1575944 | tf_op jit(solution)/shard_map/ppermute | solution.py:18
  297.0 51.4 %collective-permute-start.9 = (f32[256,513]{0,1:T(8,128)S(1)}, f32[256,513]{0,1:T(8,128)}, u32[]{:S(2)}, u32[]{:S(2)}) collective-permute-start(f32[256,513]{0,1:T(8,128)S(1)} %get-tuple-element.2280), channel_id=1, source_target_pairs={{0,16},{1,17},{2,18},{3,19},{4,20},{5,21},{6,22},{7,23},{8,24},{9,... | collective-permute-start | bytes 1575944 | tf_op jit(solution)/shard_map/ppermute | solution.py:18
  317.0 35.6 %copy-start.16 = (f32[256,513]{0,1:T(8,128)}, f32[256,513]{0,1:T(8,128)S(1)}, u32[]{:S(2)}) copy-start(f32[256,513]{0,1:T(8,128)S(1)} %fusion.243) | copy-start | bytes 1575940
  372.7 20.4 %copy-start.19 = (f32[256,513]{0,1:T(8,128)S(1)}, f32[256,513]{0,1:T(8,128)}, u32[]{:S(2)}) copy-start(f32[256,513]{0,1:T(8,128)} %copy-done.18) | copy-start | bytes 1575940
  377.6 9.4 %collective-permute-start.12 = (f32[256,513]{0,1:T(8,128)}, f32[256,513]{0,1:T(8,128)S(1)}, u32[]{:S(2)}, u32[]{:S(2)}) collective-permute-start(f32[256,513]{0,1:T(8,128)} %get-tuple-element.2281), channel_id=1, source_target_pairs={{32,0},{33,1},{34,2},{35,3},{36,4},{37,5},{38,6},{39,7},{40,8},{41... | collective-permute-start | bytes 1575944 | tf_op jit(solution)/shard_map/ppermute | solution.py:18
  379.9 13.2 %collective-permute-start.11 = (f32[256,513]{0,1:T(8,128)}, f32[256,513]{0,1:T(8,128)S(1)}, u32[]{:S(2)}, u32[]{:S(2)}) collective-permute-start(f32[256,513]{0,1:T(8,128)} %get-tuple-element.2281), channel_id=1, source_target_pairs={{0,32},{1,33},{2,34},{3,35},{4,36},{5,37},{6,38},{7,39},{8,40},{9,... | collective-permute-start | bytes 1575944 | tf_op jit(solution)/shard_map/ppermute | solution.py:18
  417.1 23.5 %copy-start.23 = (f32[256,513]{0,1:T(8,128)S(1)}, f32[256,513]{0,1:T(8,128)}, u32[]{:S(2)}) copy-start(f32[256,513]{0,1:T(8,128)} %copy-done.22) | copy-start | bytes 1575940
  422.3 13.2 %collective-permute-start.14 = (f32[256,513]{0,1:T(8,128)S(1)}, f32[256,513]{0,1:T(8,128)}, u32[]{:S(2)}, u32[]{:S(2)}) collective-permute-start(f32[256,513]{0,1:T(8,128)S(1)} %get-tuple-element.2282), channel_id=1, source_target_pairs={{64,0},{65,1},{66,2},{67,3},{68,4},{69,5},{70,6},{71,7},{72,8},{73... | collective-permute-start | bytes 1575944 | tf_op jit(solution)/shard_map/ppermute | solution.py:18
  426.7 13.8 %collective-permute-start.13 = (f32[256,513]{0,1:T(8,128)S(1)}, f32[256,513]{0,1:T(8,128)}, u32[]{:S(2)}, u32[]{:S(2)}) collective-permute-start(f32[256,513]{0,1:T(8,128)S(1)} %get-tuple-element.2282), channel_id=1, source_target_pairs={{0,64},{1,65},{2,66},{3,67},{4,68},{5,69},{6,70},{7,71},{8,72},{9,... | collective-permute-start | bytes 1575944 | tf_op jit(solution)/shard_map/ppermute | solution.py:18
  464.8 22.9 %copy-start.27 = (f32[256,513]{0,1:T(8,128)S(1)}, f32[256,513]{0,1:T(8,128)}, u32[]{:S(2)}) copy-start(f32[256,513]{0,1:T(8,128)} %copy-done.26) | copy-start | bytes 1575940
  468.6 13.4 %collective-permute-start.16 = (f32[256,513]{0,1:T(8,128)S(1)}, f32[256,513]{0,1:T(8,128)S(1)}, u32[]{:S(2)}, u32[]{:S(2)}) collective-permute-start(f32[256,513]{0,1:T(8,128)S(1)} %get-tuple-element.2283), channel_id=1, source_target_pairs={{128,0},{129,1},{130,2},{131,3},{132,4},{133,5},{134,6},{135,7},{1... | collective-permute-start | bytes 1575944 | tf_op jit(solution)/shard_map/ppermute | solution.py:18
  471.7 16.0 %collective-permute-start.15 = (f32[256,513]{0,1:T(8,128)S(1)}, f32[256,513]{0,1:T(8,128)S(1)}, u32[]{:S(2)}, u32[]{:S(2)}) collective-permute-start(f32[256,513]{0,1:T(8,128)S(1)} %get-tuple-element.2283), channel_id=1, source_target_pairs={{0,128},{1,129},{2,130},{3,131},{4,132},{5,133},{6,134},{7,135},{8... | collective-permute-start | bytes 1575944 | tf_op jit(solution)/shard_map/ppermute | solution.py:18
  511.9 9.1 %collective-permute-start.17 = (f32[256]{0:T(256)S(1)}, f32[256]{0:T(256)S(1)}, u32[]{:S(2)}, u32[]{:S(2)}) collective-permute-start(f32[256]{0:T(256)S(1)} %get-tuple-element.501), channel_id=1, source_target_pairs={{0,1},{1,2},{2,3},{3,4},{4,5},{5,6},{6,7},{7,8},{8,9},{9,10},{10,1... | collective-permute-start | bytes 3080 | tf_op jit(solution)/shard_map/ppermute | solution.py:18
  (34 other events, 332.4 us)
